TPU v7x, 32 devices: a whole 2x2x4 slice. The times are simulated.
32 devices in a mesh: dp: 4 (over x, core), fsdp: 8 (over z, y).
Axes of the slice: x: 2, y: 2, z: 4, core: 2. Of those that a mesh axis runs over, the one named last changes fastest.
Arguments:
- tokens: bfloat16 [8192, 640], P(('dp', 'fsdp')), may hold values from -6 to 6
- cotangent: bfloat16 [8192, 640], P(('dp', 'fsdp')), may hold values from -6 to 6
- masked_pos: int32 [8192], P(('dp', 'fsdp')), may hold values from 0 to 1
- labels: int32 [8192], P(('dp', 'fsdp')), may hold values from 0 to 3
- decoder: bfloat16 [4, 640], replicated, may hold values from -0.375 to 0.375
- master: float32 [640, 12800], P('fsdp'), may hold values from -0.6324555 to 0.6324555
- small_params: float32 [640, 16], P('fsdp'), may hold values from -0.8 to 1.4
- small_first: float32 [640, 16], P('fsdp'), may hold values from -128 to 128
- small_second: float32 [640, 16], P('fsdp'), may hold values from 163.84 to 4096
- block_slots: int32 [40], replicated, may hold values from 0 to 39, as said below
- first_moment: float32 [40, 640, 320], P('fsdp'), may hold values from -128 to 128
- second_moment: float32 [40, 640, 320], P('fsdp'), may hold values from 163.84 to 4096
- left_bases: float32 [40, 640, 640], P('fsdp'), may hold values from -1 to 1, as said below
- right_bases: float32 [40, 320, 320], P('fsdp'), may hold values from -1 to 1, as said below
Outputs:
- out_tokens: bfloat16 [8192, 640], P(('dp', 'fsdp'))
- grad_tokens: bfloat16 [8192, 640], P(('dp', 'fsdp'))
- grad_weights: float32 [640, 12800], P('fsdp')
- grad_small: float32 [640, 16], P('fsdp')
- new_first: float32 [40, 640, 320], P('fsdp')
- new_second: float32 [40, 640, 320], P('fsdp')
- new_master: float32 [640, 12800], P('fsdp')
- new_copy: bfloat16 [640, 12800], P('fsdp')
- new_small: float32 [640, 16], P('fsdp')
- new_small_first: float32 [640, 16], P('fsdp')
- new_small_second: float32 [640, 16], P('fsdp')
- loss_accuracy: float32 [5], replicated
- counts: int32 [4], replicated
Inputs may be any that keep to these rules, and one draw needn't show every extreme that they name: Distinct slot numbers; block b (columns b * 320 to (b + 1) * 320 - 1 of the weights) keeps its optimizer state in slot block_slots[b], held by fsdp index block_slots[b] // 5; at most 5 blocks on one index. `left_bases`: each slot's matrix is orthogonal. `right_bases`: each slot's matrix is orthogonal.
All inputs are finite; a program needn't handle non-finite values.
Results may differ from a plain program's by a relative error of at most 0.013.
The roundings to bfloat16 on the way count: a program that leaves them out, or rounds other values in their place, can miss the bound.
Values may be sent and summed in bfloat16 or wider, within the bound.
No kernel may reach another device: no remote copies, remote signals or barrier semaphores. Data moves between devices by JAX's collectives and lax.ppermute only.
A program may use at most 256 MiB of HBM per device.

v0:
```python
import jax
import jax.numpy as jnp
from jax import lax
from jax.sharding import PartitionSpec as P

HEAD_DIM = 32
SEQ_LEN = 256
STEP = 5
EPS_NORM = 1e-05
EPS_ADAM = 1e-08
BETA_FIRST = 0.5
BETA_SECOND = 0.5
RATE_MATRIX = 0.02
RATE_VECTOR = 0.05
EXACT_PRECISION = lax.Precision.HIGHEST


def normalize_layer(rows_in, norm_gain, norm_shift):
    centred = rows_in - jnp.mean(rows_in, axis=-1, keepdims=True)
    variance = jnp.mean(centred * centred, axis=-1, keepdims=True)
    return centred * lax.rsqrt(variance + EPS_NORM) * norm_gain + norm_shift


def exact_gelu(inputs):
    return jax.nn.gelu(inputs, approximate=False)


def adam_direction(first_new, second_new):
    return (
        first_new
        / (1.0 - BETA_FIRST**STEP)
        / (jnp.sqrt(second_new / (1.0 - BETA_SECOND**STEP)) + EPS_ADAM)
    )


def contract_rows(left_mat, right_mat):
    return lax.dot_general(
        left_mat, right_mat, (((0,), (0,)), ((), ())), preferred_element_type=jnp.float32
    )


def times_transpose(left_mat, right_mat):
    return lax.dot_general(
        left_mat, right_mat, (((1,), (1,)), ((), ())), preferred_element_type=jnp.float32
    )


def block_scores(queries, key_rows):
    return jnp.einsum(
        "slhd,smhd->shlm", queries, key_rows, preferred_element_type=jnp.float32
    ) * HEAD_DIM ** (-0.5)


def attend_block(weight_blocks):
    queries, key_rows, values = weight_blocks
    scores = block_scores(queries, key_rows)
    highest = jnp.max(scores, axis=-1, keepdims=True)
    exponent = jnp.exp(scores - highest)
    totals = jnp.sum(exponent, axis=-1, keepdims=True)
    weights_soft = (exponent / totals).astype(jnp.bfloat16)
    mixed_rows = jnp.einsum(
        "shlm,smhd->slhd", weights_soft, values, preferred_element_type=jnp.float32
    )
    return (mixed_rows.astype(jnp.bfloat16), (highest + jnp.log(totals))[..., 0])


def attend_back(weight_blocks):
    queries, key_rows, values, log_total, d_attended = weight_blocks
    probabilities = jnp.exp(block_scores(queries, key_rows) - log_total[..., None])
    d_values = jnp.einsum(
        "shlm,slhd->smhd",
        probabilities.astype(jnp.bfloat16),
        d_attended,
        preferred_element_type=jnp.float32,
    )
    d_probs = jnp.einsum("slhd,smhd->shlm", d_attended, values, preferred_element_type=jnp.float32)
    d_scores = (
        probabilities * (d_probs - jnp.sum(probabilities * d_probs, axis=-1, keepdims=True))
    ).astype(jnp.bfloat16)
    d_queries = jnp.einsum(
        "shlm,smhd->slhd", d_scores, key_rows, preferred_element_type=jnp.float32
    ) * HEAD_DIM ** (-0.5)
    d_keys = jnp.einsum(
        "shlm,slhd->smhd", d_scores, queries, preferred_element_type=jnp.float32
    ) * HEAD_DIM ** (-0.5)
    return (
        d_queries.astype(jnp.bfloat16),
        d_keys.astype(jnp.bfloat16),
        d_values.astype(jnp.bfloat16),
    )


def local(
    tokens,
    cotangent,
    masked_pos,
    labels,
    decoder,
    master,
    small_params,
    small_first,
    small_second,
    block_slots,
    first_moment,
    second_moment,
    left_bases,
    right_bases,
):
    model_width = decoder.shape[1]
    hidden = (master.shape[1] - 4 * model_width) // 2
    heads_count = model_width // HEAD_DIM
    token_count = tokens.shape[0]
    local_weights = master.astype(jnp.bfloat16)
    local_small = small_params.astype(jnp.bfloat16)
    weights, small_all = (
        lax.all_gather(local_weights, "fsdp", axis=0, tiled=True),
        lax.all_gather(local_small, "fsdp", axis=0, tiled=True),
    )
    params = small_all.astype(jnp.float32)
    gain_one, shift_one, bias_query, bias_value, bias_output, gain_two, shift_two, bias_down = [
        params[:, column] for column in range(8)
    ]
    bias_up = params[:, 8:].reshape(hidden)
    rows_in = tokens.astype(jnp.float32)
    normed = normalize_layer(rows_in, gain_one, shift_one).astype(jnp.bfloat16)
    bias_qkv = jnp.concatenate([bias_query, jnp.zeros_like(bias_query), bias_value])
    projected = (
        jnp.dot(normed, weights[:, : 3 * model_width], preferred_element_type=jnp.float32)
        + bias_qkv
    ).astype(jnp.bfloat16)
    seq_count = token_count // SEQ_LEN
    per_block = max(1, min(seq_count, 512 // SEQ_LEN))
    block_shape = (seq_count // per_block, per_block, SEQ_LEN, heads_count, HEAD_DIM)
    queries = projected[:, :model_width].reshape(block_shape)
    key_rows = projected[:, model_width : 2 * model_width].reshape(block_shape)
    values = projected[:, 2 * model_width :].reshape(block_shape)
    attention_result, log_total = lax.map(attend_block, (queries, key_rows, values))
    attention_result = attention_result.reshape(token_count, model_width)
    middle = (
        rows_in
        + jnp.dot(
            attention_result,
            weights[:, 3 * model_width : 4 * model_width],
            preferred_element_type=jnp.float32,
        )
        + bias_output
    )
    normed_two = normalize_layer(middle, gain_two, shift_two).astype(jnp.bfloat16)
    pre_active = (
        jnp.dot(
            normed_two,
            weights[:, 4 * model_width : 4 * model_width + hidden],
            preferred_element_type=jnp.float32,
        )
        + bias_up
    )
    active = exact_gelu(pre_active).astype(jnp.bfloat16)
    output_rows = (
        middle + times_transpose(active, weights[:, 4 * model_width + hidden :]) + bias_down
    )
    out_tokens = output_rows.astype(jnp.bfloat16)
    logits = times_transpose(out_tokens, decoder)
    log_norm = jax.nn.logsumexp(logits, axis=-1)
    one_hot = (labels[:, None] == jnp.arange(decoder.shape[0], dtype=jnp.int32)[None, :]).astype(
        jnp.float32
    )
    hidden_tokens = masked_pos.astype(jnp.float32)
    chosen = one_hot * hidden_tokens[:, None]
    entropy = log_norm - jnp.sum(one_hot * logits, axis=-1)
    right_prob = jnp.sum(one_hot * jnp.exp(logits - log_norm[:, None]), axis=-1)
    local_sums = jnp.concatenate(
        [jnp.sum(hidden_tokens * entropy)[None], jnp.sum(chosen * right_prob[:, None], axis=0)]
    )
    global_sums, global_counts = lax.psum((local_sums, jnp.sum(chosen, axis=0)), ("dp", "fsdp"))
    loss_accuracy = jnp.concatenate(
        [
            global_sums[:1] / jnp.maximum(jnp.sum(global_counts), 1.0),
            global_sums[1:] / jnp.maximum(global_counts, 1.0),
        ]
    )
    counts = global_counts.astype(jnp.int32)
    weights_back, small_back = (
        lax.all_gather(local_weights, "fsdp", axis=0, tiled=True),
        lax.all_gather(local_small, "fsdp", axis=0, tiled=True),
    )
    params_back = small_back.astype(jnp.float32)
    back_rows = cotangent.astype(jnp.float32)
    d_active = jnp.dot(
        cotangent, weights_back[:, 4 * model_width + hidden :], preferred_element_type=jnp.float32
    )
    unused, gelu_pull = jax.vjp(exact_gelu, pre_active)
    d_pre = gelu_pull(d_active)[0].astype(jnp.bfloat16)
    d_normed_two = times_transpose(
        d_pre, weights_back[:, 4 * model_width : 4 * model_width + hidden]
    )
    unused, norm_pull_two = jax.vjp(normalize_layer, middle, params_back[:, 5], params_back[:, 6])
    d_middle_norm, d_gain_two, d_shift_two = norm_pull_two(d_normed_two)
    d_middle = back_rows + d_middle_norm
    d_branch = d_middle.astype(jnp.bfloat16)
    d_attended = times_transpose(
        d_branch, weights_back[:, 3 * model_width : 4 * model_width]
    ).astype(jnp.bfloat16)
    d_queries, d_keys, d_values = lax.map(
        attend_back, (queries, key_rows, values, log_total, d_attended.reshape(block_shape))
    )
    d_projected = jnp.concatenate(
        [
            d_queries.reshape(token_count, model_width),
            d_keys.reshape(token_count, model_width),
            d_values.reshape(token_count, model_width),
        ],
        axis=1,
    )
    d_normed = times_transpose(d_projected, weights_back[:, : 3 * model_width])
    unused, norm_pull_one = jax.vjp(normalize_layer, rows_in, params_back[:, 0], params_back[:, 1])
    d_rows_norm, d_gain_one, d_shift_one = norm_pull_one(d_normed)
    grad_tokens = (d_middle + d_rows_norm).astype(jnp.bfloat16)
    grad_w_local = jnp.concatenate(
        [
            contract_rows(normed, d_projected),
            contract_rows(attention_result, d_branch),
            contract_rows(normed_two, d_pre),
            contract_rows(cotangent, active),
        ],
        axis=1,
    )
    proj_sums = jnp.sum(d_projected.astype(jnp.float32), axis=0)
    small_cols = jnp.stack(
        [
            d_gain_one,
            d_shift_one,
            proj_sums[:model_width],
            proj_sums[2 * model_width :],
            jnp.sum(d_branch.astype(jnp.float32), axis=0),
            d_gain_two,
            d_shift_two,
            jnp.sum(back_rows, axis=0),
        ],
        axis=1,
    )
    grad_s_local = jnp.concatenate(
        [small_cols, jnp.sum(d_pre.astype(jnp.float32), axis=0).reshape(model_width, -1)], axis=1
    )
    part_w, part_s = (
        lax.psum_scatter(grad_w_local, "dp", scatter_dimension=1, tiled=True),
        lax.psum_scatter(grad_s_local, "dp", scatter_dimension=1, tiled=True),
    )
    part_w, part_s = (
        lax.psum_scatter(part_w, "fsdp", scatter_dimension=0, tiled=True),
        lax.psum_scatter(part_s, "fsdp", scatter_dimension=0, tiled=True),
    )
    grad_w, grad_s = (
        lax.all_gather(part_w, "dp", axis=1, tiled=True),
        lax.all_gather(part_s, "dp", axis=1, tiled=True),
    )
    row_count = grad_w.shape[0]
    block_width = model_width // 2
    block_count = grad_w.shape[1] // block_width
    owned_slots = first_moment.shape[0]
    devices = lax.axis_size("fsdp")
    slot_ids = jnp.arange(owned_slots * devices, dtype=jnp.int32)
    matches = block_slots[None, :] == slot_ids[:, None]
    in_use = jnp.any(matches, axis=1)
    source_block = jnp.sum(
        jnp.where(matches, jnp.arange(block_count, dtype=jnp.int32)[None, :], 0), axis=1
    )
    outgoing = jnp.take(grad_w.reshape(row_count, block_count, block_width), source_block, axis=1)
    outgoing = jnp.where(in_use[None, :, None], outgoing, 0.0).reshape(
        row_count, devices, owned_slots, block_width
    )
    incoming = lax.all_to_all(outgoing, "fsdp", split_axis=1, concat_axis=0, tiled=True).reshape(
        row_count * devices, owned_slots, block_width
    )
    my_use = lax.dynamic_slice_in_dim(in_use, lax.axis_index("fsdp") * owned_slots, owned_slots)
    eigen_turned = jnp.einsum("kdi,dkc->kic", left_bases, incoming, precision=EXACT_PRECISION)
    eigen_turned = jnp.einsum("kic,kcj->kij", eigen_turned, right_bases, precision=EXACT_PRECISION)
    first_new = BETA_FIRST * first_moment + (1.0 - BETA_FIRST) * eigen_turned
    second_new = BETA_SECOND * second_moment + (1.0 - BETA_SECOND) * eigen_turned * eigen_turned
    direction = adam_direction(first_new, second_new)
    rotated_gradient = jnp.einsum("kij,klj->kil", direction, right_bases, precision=EXACT_PRECISION)
    rotated_gradient = jnp.einsum(
        "kdi,kil->dkl", left_bases, rotated_gradient, precision=EXACT_PRECISION
    )
    returned = lax.all_to_all(
        rotated_gradient.reshape(devices, row_count, owned_slots, block_width),
        "fsdp",
        split_axis=0,
        concat_axis=0,
        tiled=True,
    )
    by_slot = jnp.moveaxis(returned, 1, 0).reshape(row_count, devices * owned_slots, block_width)
    update = jnp.take(by_slot, block_slots, axis=1).reshape(row_count, block_count * block_width)
    new_master = master - RATE_MATRIX * update
    new_copy = new_master.astype(jnp.bfloat16)
    keep_slot = my_use[:, None, None]
    new_first = jnp.where(keep_slot, first_new, 0.0)
    new_second = jnp.where(keep_slot, second_new, 0.0)
    new_small_first = BETA_FIRST * small_first + (1.0 - BETA_FIRST) * grad_s
    new_small_second = BETA_SECOND * small_second + (1.0 - BETA_SECOND) * grad_s * grad_s
    new_small = small_params - RATE_VECTOR * adam_direction(new_small_first, new_small_second)
    return (
        out_tokens,
        grad_tokens,
        grad_w,
        grad_s,
        new_first,
        new_second,
        new_master,
        new_copy,
        new_small,
        new_small_first,
        new_small_second,
        loss_accuracy,
        counts,
    )


def solution(mesh):
    return jax.shard_map(
        local,
        mesh=mesh,
        in_specs=(
            P(("dp", "fsdp"), None),
            P(("dp", "fsdp"), None),
            P(("dp", "fsdp")),
            P(("dp", "fsdp")),
            P(),
            P("fsdp", None),
            P("fsdp", None),
            P("fsdp", None),
            P("fsdp", None),
            P(),
            P("fsdp", None, None),
            P("fsdp", None, None),
            P("fsdp", None, None),
            P("fsdp", None, None),
        ),
        out_specs=(
            P(("dp", "fsdp"), None),
            P(("dp", "fsdp"), None),
            P("fsdp", None),
            P("fsdp", None),
            P("fsdp", None, None),
            P("fsdp", None, None),
            P("fsdp", None),
            P("fsdp", None),
            P("fsdp", None),
            P("fsdp", None),
            P("fsdp", None),
            P(),
            P(),
        ),
        check_vma=False,
    )
```

profile of v0, /device:TPU:0, one launch (start us, length us, event | category | flops | bytes accessed | tf_op | source)
XLA Modules:
  0.0 1169.3 jit_solution(2485766205392647652)
XLA Ops:
  7.3 3.8 convert_element_type.121
  11.2 33.4 %all-gather = bf16[8,80,16]{1,2,0:T(8,128)(2,1)S(1)} all-gather(bf16[1,80,16]{1,2,0:T(8,128)(2,1)S(1)} %convert_bitcast_fusion), channel_id=1, replica_groups=mesh['dp'=4,'fsdp'=8] {'fsdp'}, dimensions={0}, use_global_device_ids=true | all-gather | bytes 23040 | tf_op jit(solution)/shard_map/all_gather | solution.py:117
  46.0 190.6 %all-gather.5.cloned.1.call-done = bf16[640,12800]{1,0:T(8,128)(2,1)} async-done(((bf16[80,12800]{1,0:T(8,128)(2,1)}), bf16[640,12800]{1,0:T(8,128)(2,1)}) %all-gather.5.cloned.1.call-update) | async-done | bytes 16384016 | tf_op jit(solution)/shard_map/all_gather | solution.py:116
  236.6 2.8 fusion.29
  239.4 0.9 fusion.87
  240.5 1.3 copy.111
  241.8 2.0 copy.110
  243.8 0.9 multiply_reduce_fusion.1
  244.7 0.9 fusion.15
  245.7 1.1 fusion.45
  247.3 1.9 slice-done.3
  249.2 1.4 slice-done.4
  250.6 1.1 slice-done.5
  252.5 15.0 %multiply_convert_fusion.1 = (bf16[256,5120]{1,0:T(8,128)(2,1)}, f32[256,5120]{1,0:T(8,128)}, f32[256,5120]{1,0:T(8,128)}) fusion(f32[5120]{0:T(1024)S(1)} %add.172, bf16[640,12800]{1,0:T(8,128)(2,1)S(1)} %bitcast.115, f32[256,640]{1,0:T(8,128)S(1)} %get-tuple-element.106, f32[640]{0:T(1024)S(1)} %get-tuple-element.67, f32[640]{0:T(1024)S(1)} %get-tuple-element.68, ...), kind=kOutput, calls=%fused_computation.21 | convolution fusion | flops 1765048320 | bytes 20346880 | tf_op jit(solution)/shard_map/dot_general | solution.py:150
  267.5 6.6 convert_reduce_fusion
  274.1 2.4 multiply_reduce_fusion.2
  276.9 0.9 copy-done.6
  278.0 1.6 fusion.92
  279.5 1.2 convolution_convert_fusion
  280.7 1.9 copy.115
  282.6 3.7 fusion.48
  286.9 1.4 multiply_reduce_fusion
  288.3 1.4 multiply_convert_fusion
  291.4 6.7 fusion.80
  298.1 6.6 convolution_bitcast_fusion
  304.7 3.3 fusion.76
  308.0 21.8 %pad_maximum_fusion = f32[640,12800]{1,0:T(8,128)} fusion(f32[640,5120]{1,0:T(8,128)} %convolution_bitcast_fusion, f32[640,5120]{1,0:T(8,128)} %fusion.80, f32[640,640]{1,0:T(8,128)S(1)} %copy-done.5, f32[640,1920]{1,0:T(8,128)} %fusion.76), kind=kLoop, calls=%fused_computation.2 | loop fusion | flops 24576000 | bytes 65536000 | tf_op jit(solution)/shard_map/concatenate | solution.py:218
  329.9 225.7 %reduce-scatter.5.cloned.1.call-done = f32[640,3200]{1,0:T(8,128)} async-done(((f32[640,12800]{1,0:T(8,128)}), f32[640,3200]{1,0:T(8,128)}) %reduce-scatter.5.cloned.1.call-update) | async-done | bytes 8192016 | tf_op jit(solution)/shard_map/reduce_scatter | solution.py:245
  555.7 149.0 %reduce-scatter.7.cloned.1.call-done = f32[80,3200]{1,0:T(8,128)} async-done(((f32[640,3200]{1,0:T(8,128)}), f32[80,3200]{1,0:T(8,128)}) %reduce-scatter.7.cloned.1.call-update) | async-done | bytes 1024016 | tf_op jit(solution)/shard_map/reduce_scatter | solution.py:249
  705.0 34.2 %all-gather.7.cloned.1.call-done = f32[80,12800]{1,0:T(8,128)} async-done(((f32[80,3200]{1,0:T(8,128)}), f32[80,12800]{1,0:T(8,128)}) %all-gather.7.cloned.1.call-update) | async-done | bytes 4096016 | tf_op jit(solution)/shard_map/all_gather | solution.py:253
  739.2 5.7 reshape.267
  744.9 5.5 copy.130
  750.4 5.5 gather_fusion
  755.9 5.6 bitcast_select_fusion
  761.6 5.5 all-to-all-start
  767.1 109.1 %all-to-all-done = f32[80,8,5,320]{3,0,2,1:T(8,128)} async-done(((f32[80,8,5,320]{3,0,2,1:T(8,128)}), f32[80,8,5,320]{3,0,2,1:T(8,128)}, u32[]{:S(2)}, u32[]{:S(2)}) %all-to-all-start) | async-done | bytes 4096032 | tf_op jit(solution)/shard_map/all_to_all | solution.py:271
  876.2 2.8 copy.131
  879.0 33.4 %fusion.93 = f32[5,320,640]{2,1,0:T(8,128)S(1)} fusion(f32[640,5,320]{2,0,1:T(8,128)S(1)} %bitcast.89, f32[5,640,640]{2,1,0:T(8,128)} %param.28), kind=kOutput, calls=%fused_computation.168 | convolution fusion | flops 7864320000 | bytes 16384000 | tf_op jit(solution)/shard_map/kdi,dkc->kic/dot_general | solution.py:275
  912.4 18.5 %broadcast_select_fusion = (f32[5,640,320]{1,2,0:T(8,128)}, f32[5,640,320]{1,2,0:T(8,128)}, f32[5,640,320]{1,2,0:T(8,128)}) fusion(pred[5]{0:T(512)(128)(4,1)S(1)} %dynamic_slice.21, f32[5,640,320]{1,2,0:T(8,128)} %param.27, f32[5,640,320]{1,2,0:T(8,128)} %param.26, f32[5,320,640]{2,1,0:T(8,128)S(1)} %fusion.93, f32[5,320,320]{2,1,0:T(8,128)S(1)} %copy-done), kind=kOutput, calls=%fused_computation.61 | convolution fusion | flops 3940352000 | bytes 26624004 | tf_op jit(solution)/shard_map/kic,kcj->kij/dot_general | solution.py:276
  930.9 19.0 %fusion.17 = f32[5,640,320]{1,2,0:T(8,128)S(1)} fusion(f32[5,320,320]{2,1,0:T(8,128)S(1)} %copy-done, f32[5,640,320]{1,2,0:T(8,128)} %get-tuple-element.114, f32[5,640,320]{1,2,0:T(8,128)} %param.26, f32[5,640,320]{1,2,0:T(8,128)} %param.27), kind=kOutput, calls=%fused_computation.42 | convolution fusion | flops 3942400000 | bytes 18432000 | tf_op jit(solution)/shard_map/kij,klj->kil/dot_general | solution.py:280
  950.0 20.1 %convolution_bitcast_fusion.1 = f32[640,5,320]{0,2,1:T(8,128)} fusion(f32[5,640,320]{1,2,0:T(8,128)S(1)} %fusion.17, f32[5,640,640]{2,1,0:T(8,128)S(1)} %bitcast.87), kind=kOutput, calls=%fused_computation.58 | convolution fusion | flops 7864320000 | bytes 16384000 | tf_op jit(solution)/shard_map/kdi,kil->dkl/dot_general | solution.py:281
  970.2 6.6 copy.134
  976.7 4.9 copy.135
  981.7 4.7 all-to-all-start.1
  988.0 0.9 reshape.266
  989.8 0.9 stack.38
  991.6 1.6 convert_reduce_fusion.1
  994.0 3.1 fusion.81
  997.6 1.1 convert_reduce_fusion.3
  998.8 0.9 stack.39
  1002.3 2.3 concatenate.21
  1004.6 15.0 %all-reduce = f32[640,16]{1,0:T(8,128)} all-reduce(f32[640,16]{1,0:T(8,128)S(1)} %concatenate.21), channel_id=4, replica_groups=mesh['dp'=4,'fsdp'=8] {'dp'}, use_global_device_ids=true, to_apply=%region_21.22.clone | all-reduce | flops 10240 | bytes 81920
  1019.6 1.8 constant_dynamic-slice_fusion
  1021.5 5.9 fusion.42
  1029.3 88.3 %all-reduce.1 = (f32[4]{0:T(128)S(1)}, f32[5]{0:T(128)S(1)}) all-reduce(f32[4]{0:T(128)S(1)} %get-tuple-element.77, f32[5]{0:T(128)S(1)} %pad_maximum_fusion.3), channel_id=1, replica_groups=mesh['dp'=4,'fsdp'=8] {'dp','fsdp'}, use_global_device_ids=true, to_apply=%region_33.35 | all-reduce | flops 9 | bytes 72 | tf_op jit(solution)/shard_map/psum | solution.py:174
  1117.6 1.1 fusion.89
  1120.0 8.9 reduce-scatter.9.cloned.1.call-done
  1129.7 5.2 all-gather.1
  1135.5 5.5 gather_fusion.1
  1141.0 3.0 bitcast_multiply_fusion
  1144.1 3.7 copy.136
  1147.8 5.5 mul.298
  1153.3 6.7 fusion.83
  1160.0 2.0 copy.148
  (153 shorter events, 17.4 us)
Async XLA Ops:
  7.2 905.2 %copy-start = (f32[5,320,320]{2,1,0:T(8,128)S(1)}, f32[5,320,320]{2,1,0:T(8,128)}, u32[]{:S(2)}) copy-start(f32[5,320,320]{2,1,0:T(8,128)} %param.29) | copy-start | bytes 6144004
  7.2 4.0 copy-start.25
  7.2 38.5 %copy-start.4 = (bf16[256,640]{1,0:T(8,128)(2,1)S(1)}, bf16[256,640]{1,0:T(8,128)(2,1)}, u32[]{:S(2)}) copy-start(bf16[256,640]{1,0:T(8,128)(2,1)} %param.16) | copy-start | bytes 983044
  7.2 229.4 %all-gather.5.cloned.1.call-start = ((), (), s32[]{:S(2)}) async-start(), calls=%async_computation.5 | async-start | bytes 18432000 | tf_op jit(solution)/shard_map/all_gather | solution.py:116
  11.1 544.6 %reduce-scatter.5.cloned.1.call-start = ((), (), s32[]{:S(2)}) async-start(), calls=%async_computation.6 | async-start | bytes 40960000 | tf_op jit(solution)/shard_map/reduce_scatter | solution.py:245
  46.0 198.6 %copy-start.27 = (f32[256]{0:T(256)}, f32[256]{0:T(256)S(1)}, u32[]{:S(2)}) copy-start(f32[256]{0:T(256)S(1)} %fusion.63) | copy-start | bytes 3076
  240.5 5.1 copy-start.12
  241.7 3.9 copy-start.14
  243.8 1.9 copy-start.22
  243.8 3.6 slice-start.2
  244.7 2.7 copy-start.1
  244.7 4.5 slice-start.3
  245.6 4.9 slice-start.4
  245.7 6.0 slice-start.5
  252.5 15.0 %copy-start.16 = (bf16[256,640]{1,0:T(8,128)(2,1)S(1)}, bf16[256,640]{1,0:T(8,128)(2,1)}, u32[]{:S(2)}) copy-start(bf16[256,640]{1,0:T(8,128)(2,1)} %param.17) | copy-start | bytes 983044
  274.1 2.4 copy-start.19
  276.9 0.9 copy-start.6
  282.6 4.1 copy-start.2
  282.6 4.2 copy-start.9
  282.6 4.3 copy-start.23
  286.9 17.8 %copy-start.8 = (bf16[20,32,256]{2,1,0:T(8,128)(2,1)}, bf16[20,32,256]{2,1,0:T(8,128)(2,1)S(1)}, u32[]{:S(2)}) copy-start(bf16[20,32,256]{2,1,0:T(8,128)(2,1)S(1)} %fusion.48) | copy-start | bytes 983044
  288.2 1.4 copy-start.15
  288.2 2.3 copy-start.13
  289.7 1.7 copy-start.20
  290.6 14.1 %copy-start.10 = (bf16[20,32,256]{2,1,0:T(8,128)(2,1)}, bf16[20,32,256]{2,1,0:T(8,128)(2,1)S(1)}, u32[]{:S(2)}) copy-start(bf16[20,32,256]{2,1,0:T(8,128)(2,1)S(1)} %fusion.47) | copy-start | bytes 983044
  291.4 13.3 %copy-start.11 = (bf16[20,32,256]{2,1,0:T(8,128)(2,1)}, bf16[20,32,256]{2,1,0:T(8,128)(2,1)S(1)}, u32[]{:S(2)}) copy-start(bf16[20,32,256]{2,1,0:T(8,128)(2,1)S(1)} %fusion.46) | copy-start | bytes 983044
  291.4 6.7 copy-start.17
  291.4 6.7 copy-start.21
  304.7 3.3 copy-start.5
  329.9 374.9 %copy-start.35 = (s32[40]{0:T(128)S(1)}, s32[40]{0:T(128)}, u32[]{:S(2)}) copy-start(s32[40]{0:T(128)} %param.25) | copy-start | bytes 484
  329.9 374.8 %reduce-scatter.7.cloned.1.call-start = ((), (), s32[]{:S(2)}) async-start(), calls=%async_computation.7 | async-start | bytes 9216000 | tf_op jit(solution)/shard_map/reduce_scatter | solution.py:249
  555.7 183.5 %all-gather.7.cloned.1.call-start = ((), (), s32[]{:S(2)}) async-start(), calls=%async_computation.8 | async-start | bytes 5120000 | tf_op jit(solution)/shard_map/all_gather | solution.py:253
  761.6 114.7 %all-to-all-start = ((f32[80,8,5,320]{3,0,2,1:T(8,128)}), f32[80,8,5,320]{3,0,2,1:T(8,128)}, u32[]{:S(2)}, u32[]{:S(2)}) async-start(f32[80,8,5,320]{3,0,2,1:T(8,128)} %bitcast.88), calls=%async_computation.3 | async-start | bytes 9830400 | tf_op jit(solution)/shard_map/all_to_all | solution.py:271
  879.0 71.0 %slice-start = ((s8[8192000]{0:T(1024)(128)(4,1)}), s8[4194304]{0:T(1024)(128)(4,1)S(1)}, s32[]{:S(2)}) async-start(s8[8192000]{0:T(1024)(128)(4,1)} %bitcast.86), calls=%async_computation.10 | async-start | bytes 8388608
  912.4 37.6 %slice-start.1 = ((s8[8192000]{0:T(1024)(128)(4,1)}), s8[3997696]{0:T(1024)(128)(4,1)S(1)}, s32[]{:S(2)}) async-start(s8[8192000]{0:T(1024)(128)(4,1)} %bitcast.86), calls=%async_computation.11 | async-start | bytes 7995392
  981.7 5.0 copy-start.32
  981.7 5.0 copy-start.36
  981.7 153.8 %all-to-all-start.1 = ((f32[8,80,5,320]{3,1,2,0:T(8,128)}), f32[8,80,5,320]{3,1,2,0:T(8,128)}, u32[]{:S(2)}, u32[]{:S(2)}) async-start(f32[8,80,5,320]{3,1,2,0:T(8,128)} %copy.135), calls=%async_computation.4 | async-start | bytes 9830400 | tf_op jit(solution)/shard_map/all_to_all | solution.py:284
  986.4 142.4 %reduce-scatter.9.cloned.1.call-start = ((), (), s32[]{:S(2)}) async-start(), calls=%async_computation.9 | async-start | bytes 368640 | tf_op jit(solution)/shard_map/reduce_scatter | solution.py:250
  988.9 8.3 copy-start.28
  991.6 6.1 copy-start.7
  991.6 6.1 copy-start.18
  997.2 24.3 %copy-start.34 = (f32[640]{0:T(1024)S(1)}, f32[640]{0:T(1024)}, u32[]{:S(2)}) copy-start(f32[640]{0:T(1024)} %get-tuple-element.66) | copy-start | bytes 7684
  1021.5 6.0 copy-start.31
  1021.5 6.3 copy-start.33
  1021.5 113.4 %copy-start.26 = (f32[80,16]{0,1:T(8,128)S(1)}, f32[80,16]{0,1:T(8,128)}, u32[]{:S(2)}) copy-start(f32[80,16]{0,1:T(8,128)} %param.22) | copy-start | bytes 15364
  1021.5 113.4 %copy-start.29 = (f32[80,16]{0,1:T(8,128)S(1)}, f32[80,16]{0,1:T(8,128)}, u32[]{:S(2)}) copy-start(f32[80,16]{0,1:T(8,128)} %param.23) | copy-start | bytes 15364
  1021.5 113.4 %copy-start.30 = (f32[80,16]{0,1:T(8,128)S(1)}, f32[80,16]{0,1:T(8,128)}, u32[]{:S(2)}) copy-start(f32[80,16]{0,1:T(8,128)} %param.24) | copy-start | bytes 15364
  1027.5 116.6 %copy-start.24 = (bf16[256,640]{1,0:T(8,128)(2,1)}, bf16[256,640]{1,0:T(8,128)(2,1)S(1)}, u32[]{:S(2)}) copy-start(bf16[256,640]{1,0:T(8,128)(2,1)S(1)} %fusion.42) | copy-start | bytes 983044
  1153.3 6.7 copy-start.3
Sparse Core Ops, SparseCore 0:
  11.2 225.3 all-gather.4
  330.0 225.6 reduce-scatter.4
  559.4 145.2 reduce-scatter.6
  706.1 32.9 all-gather.6
  1021.6 107.2 reduce-scatter.8
where the time goes:
time: 1180 us; the launch traced here: 1170 us
  waiting for transfers between devices  717 us (61%)
  matrix products  156 us (13%)
  blocking collectives  142 us (12%)
  local copies, waits for them, and re-layouts  76.1 us (6%)
  other arithmetic  51.6 us (4%)
  between operations  16 us (1%)
    reduce_scatter x1, waiting for transfers between devices, local(): lax.psum_scatter(grad_w_local, 'dp', scatter_dimension=1, tiled=True)  226 us
    all_gather x1, waiting for transfers between devices, local(): lax.all_gather(local_weights, 'fsdp', axis=0, tiled=True)  191 us
    reduce_scatter x1, waiting for transfers between devices, local(): lax.psum_scatter(part_w, 'fsdp', scatter_dimension=0, tiled=True)  149 us
    all_to_all x1, waiting for transfers between devices, local(): lax.all_to_all(outgoing, 'fsdp', split_axis=1, concat_axis=0, tiled=True)  109 us
    psum x1, blocking collectives, local(): lax.psum((local_sums, jnp.sum(chosen, axis=0)), ('dp', 'fsdp'))  88.3 us
    all_gather x1, waiting for transfers between devices, local(): lax.all_gather(part_w, 'dp', axis=1, tiled=True)  34.2 us
    all_gather x1, blocking collectives, local(): lax.all_gather(local_small, 'fsdp', axis=0, tiled=True)  33.4 us
    dot_general x1, matrix products, local(): jnp.einsum('kdi,dkc->kic', left_bases, incoming, precision=EXACT_PRECISION)  33.4 us
  transfers between devices with their start and end apart: 7, of which 6 were waited for; matrix products, arithmetic and copies ran while one was open for 3% of the time, Pallas kernels for 0%

commit v1 on v0

--- a/solution.py
+++ b/solution.py
@@ -13,6 +13,19 @@
 RATE_MATRIX = 0.02
 RATE_VECTOR = 0.05
 EXACT_PRECISION = lax.Precision.HIGHEST
+
+
+def collect(shard, axis, dim):
+    ways = lax.axis_size(axis)
+    up = [(d, (d + 1) % ways) for d in range(ways)]
+    down = [(d, (d - 1) % ways) for d in range(ways)]
+    earlier, later = ([shard], [shard])
+    for _ in range(ways // 2):
+        earlier.append(lax.ppermute(earlier[-1], axis, up))
+    for _ in range((ways - 1) // 2):
+        later.append(lax.ppermute(later[-1], axis, down))
+    line = jnp.concatenate([*earlier[::-1], *later[1:]], axis=dim)
+    return jnp.roll(line, (lax.axis_index(axis) - ways // 2) * shard.shape[dim], axis=dim)
 
 
 def normalize_layer(rows_in, norm_gain, norm_shift):
@@ -113,7 +126,7 @@
     local_weights = master.astype(jnp.bfloat16)
     local_small = small_params.astype(jnp.bfloat16)
     weights, small_all = (
-        lax.all_gather(local_weights, "fsdp", axis=0, tiled=True),
+        collect(local_weights, "fsdp", 0),
         lax.all_gather(local_small, "fsdp", axis=0, tiled=True),
     )
     params = small_all.astype(jnp.float32)

time: 1180 us -> 1540 us (1.31)
  waiting for transfers between devices: 717 us -> 889 us
  blocking collectives: 142 us -> 267 us
  local copies, waits for them, and re-layouts: 76.1 us -> 106 us
  starting transfers between devices: 10.6 us -> 26.3 us
    ppermute x0 -> x7, waiting for transfers between devices: none -> 280 us  [the longest x4 215 us: collect(): earlier.append(lax.ppermute(earlier[-1], axis, up))]
    all_gather x1, waiting for transfers between devices: 191 us -> 19.3 us  [local(): lax.all_gather(local_weights, 'fsdp', axis=0, tiled=True)]
    all_gather x1, blocking collectives: 33.4 us -> 130 us  [local(): lax.all_gather(local_small, 'fsdp', axis=0, tiled=True)]
    reduce_scatter x1, waiting for transfers between devices: 8.85 us -> 61.2 us  [local(): lax.psum_scatter(part_s, 'fsdp', scatter_dimension=0, tiled=True)]
    unnamed x91 -> x120, local copies, waits for them, and re-layouts: 12.7 us -> 43.6 us
    psum x1, blocking collectives: 88.3 us -> 117 us  [local(): lax.psum((local_sums, jnp.sum(chosen, axis=0)), ('dp', 'fsdp'))]
  transfers between devices with their start and end apart: 7 -> 14, of which waited for: 6 -> 10; matrix products, arithmetic and copies ran while one was open for 3% -> 7% of each run, Pallas kernels for 0% -> 0%
where the time goes in v1:
time: 1540 us; the launch traced here: 1530 us
  waiting for transfers between devices  889 us (58%)
  blocking collectives  267 us (17%)
  matrix products  171 us (11%)
  local copies, waits for them, and re-layouts  106 us (7%)
  other arithmetic  53.3 us (3%)
  starting transfers between devices  26.3 us (2%)
  between operations  16.5 us (1%)
    reduce_scatter x1, waiting for transfers between devices, local(): lax.psum_scatter(grad_w_local, 'dp', scatter_dimension=1, tiled=True)  236 us
    ppermute x4, waiting for transfers between devices, collect(): earlier.append(lax.ppermute(earlier[-1], axis, up))  215 us
    reduce_scatter x1, waiting for transfers between devices, local(): lax.psum_scatter(part_w, 'fsdp', scatter_dimension=0, tiled=True)  149 us
    all_gather x1, blocking collectives, local(): lax.all_gather(local_small, 'fsdp', axis=0, tiled=True)  130 us
    psum x1, blocking collectives, local(): lax.psum((local_sums, jnp.sum(chosen, axis=0)), ('dp', 'fsdp'))  117 us
    all_to_all x1, waiting for transfers between devices, local(): lax.all_to_all(outgoing, 'fsdp', split_axis=1, concat_axis=0, tiled=True)  109 us
    ppermute x3, waiting for transfers between devices, collect(): later.append(lax.ppermute(later[-1], axis, down))  65.4 us
    reduce_scatter x1, waiting for transfers between devices, local(): lax.psum_scatter(part_s, 'fsdp', scatter_dimension=0, tiled=True)  61.2 us
  transfers between devices with their start and end apart: 14, of which 10 were waited for; matrix products, arithmetic and copies ran while one was open for 7% of the time, Pallas kernels for 0%

profile of v1, /device:TPU:0, one launch (start us, length us, event | category | flops | bytes accessed | tf_op | source)
XLA Modules:
  0.0 1528.3 jit_solution(1051537121998559756)
XLA Ops:
  7.3 3.8 convert_element_type.121
  11.1 3.0 collective-permute-start
  14.1 47.8 %collective-permute-done = bf16[80,12800]{1,0:T(8,128)(2,1)S(1)} collective-permute-done((bf16[80,12800]{1,0:T(8,128)(2,1)}, bf16[80,12800]{1,0:T(8,128)(2,1)S(1)}, u32[]{:S(2)}, u32[]{:S(2)}) %collective-permute-start) | collective-permute-done | bytes 2048032 | tf_op jit(solution)/shard_map/ppermute | solution.py:24
  63.2 4.7 collective-permute-start.4
  67.9 82.7 %collective-permute-done.1 = bf16[80,12800]{1,0:T(8,128)(2,1)S(1)} collective-permute-done((bf16[80,12800]{1,0:T(8,128)(2,1)S(1)}, bf16[80,12800]{1,0:T(8,128)(2,1)S(1)}, u32[]{:S(2)}, u32[]{:S(2)}) %collective-permute-start.1) | collective-permute-done | bytes 2048032 | tf_op jit(solution)/shard_map/ppermute | solution.py:24
  151.9 2.5 collective-permute-start.2
  154.4 2.2 collective-permute-start.5
  156.6 84.3 %collective-permute-done.2 = bf16[80,12800]{1,0:T(8,128)(2,1)} collective-permute-done((bf16[80,12800]{1,0:T(8,128)(2,1)S(1)}, bf16[80,12800]{1,0:T(8,128)(2,1)}, u32[]{:S(2)}, u32[]{:S(2)}) %collective-permute-start.2) | collective-permute-done | bytes 2048032 | tf_op jit(solution)/shard_map/ppermute | solution.py:24
  241.0 2.6 collective-permute-start.3
  243.7 129.9 %all-gather = bf16[8,80,16]{1,2,0:T(8,128)(2,1)S(1)} all-gather(bf16[1,80,16]{1,2,0:T(8,128)(2,1)S(1)} %convert_bitcast_fusion), channel_id=1, replica_groups=mesh['dp'=4,'fsdp'=8] {'fsdp'}, dimensions={0}, use_global_device_ids=true | all-gather | bytes 23040 | tf_op jit(solution)/shard_map/all_gather | solution.py:130
  375.2 3.2 constant_dynamic-update-slice_fusion.15
  378.4 3.2 constant_dynamic-update-slice_fusion.14
  386.0 3.0 constant_dynamic-update-slice_fusion.10
  389.0 3.1 constant_dynamic-update-slice_fusion.9
  392.1 65.4 %collective-permute-done.6 = bf16[80,12800]{1,0:T(8,128)(2,1)S(1)} collective-permute-done((bf16[80,12800]{1,0:T(8,128)(2,1)}, bf16[80,12800]{1,0:T(8,128)(2,1)S(1)}, u32[]{:S(2)}, u32[]{:S(2)}) %collective-permute-start.6) | collective-permute-done | bytes 2048032 | tf_op jit(solution)/shard_map/ppermute | solution.py:26
  458.9 3.0 constant_dynamic-update-slice_fusion.7
  461.9 3.0 constant_dynamic-update-slice_fusion.6
  467.8 1.6 constant_dynamic-update-slice_fusion.3
  469.4 3.1 constant_dynamic-update-slice_fusion.2
  472.5 3.0 constant_dynamic-update-slice_fusion.1
  477.0 2.8 fusion.33
  486.2 2.1 fusion.95
  488.5 18.4 %multiply_convert_fusion.1 = (bf16[256,5120]{1,0:T(8,128)(2,1)S(1)}, f32[256,5120]{1,0:T(8,128)}, f32[256,5120]{1,0:T(8,128)}) fusion(f32[5120]{0:T(1024)S(1)} %add.185, bf16[1280,12800]{1,0:T(8,128)(2,1)} %constant_dynamic-update-slice_fusion, s32[]{:T(128)S(6)} %select_n.49, s32[]{:T(128)S(6)} %add.222, f32[256,640]{1,0:T(8,128)S(1)} %get-tuple-element.106, ...), kind=kOutput, calls=%fused_computation.22 | convolution fusion | flops 1765048320 | bytes 20343816 | tf_op jit(solution)/shard_map/dot_general | solution.py:163
  508.4 6.7 convolution_bitcast_fusion
  515.1 19.3 %all-gather.5.cloned.1.call-done = bf16[640,12800]{1,0:T(8,128)(2,1)} async-done(((bf16[80,12800]{1,0:T(8,128)(2,1)}), bf16[640,12800]{1,0:T(8,128)(2,1)}) %all-gather.5.cloned.1.call-update) | async-done | bytes 16384016 | tf_op jit(solution)/shard_map/all_gather | solution.py:196
  534.4 9.6 convert_reduce_fusion
  544.1 6.2 multiply_reduce_fusion.2
  552.3 2.3 convolution_convert_fusion
  554.7 1.9 copy.115
  556.5 3.7 fusion.52
  560.3 4.0 multiply_reduce_fusion
  567.6 6.7 fusion.85
  574.7 3.2 fusion.81
  578.0 21.6 %pad_maximum_fusion = f32[640,12800]{1,0:T(8,128)} fusion(f32[640,5120]{1,0:T(8,128)} %convolution_bitcast_fusion, f32[640,5120]{1,0:T(8,128)} %fusion.85, f32[640,640]{1,0:T(8,128)S(1)} %fusion.97, f32[640,1920]{1,0:T(8,128)} %fusion.81), kind=kLoop, calls=%fused_computation.2 | loop fusion | flops 24576000 | bytes 65536000 | tf_op jit(solution)/shard_map/concatenate | solution.py:231
  599.7 235.6 %reduce-scatter.5.cloned.1.call-done = f32[640,3200]{1,0:T(8,128)} async-done(((f32[640,12800]{1,0:T(8,128)}), f32[640,3200]{1,0:T(8,128)}) %reduce-scatter.5.cloned.1.call-update) | async-done | bytes 8192016 | tf_op jit(solution)/shard_map/reduce_scatter | solution.py:258
  835.4 148.9 %reduce-scatter.7.cloned.1.call-done = f32[80,3200]{1,0:T(8,128)} async-done(((f32[640,3200]{1,0:T(8,128)}), f32[80,3200]{1,0:T(8,128)}) %reduce-scatter.7.cloned.1.call-update) | async-done | bytes 1024016 | tf_op jit(solution)/shard_map/reduce_scatter | solution.py:262
  984.6 34.2 %all-gather.7.cloned.1.call-done = f32[80,12800]{1,0:T(8,128)} async-done(((f32[80,3200]{1,0:T(8,128)}), f32[80,12800]{1,0:T(8,128)}) %all-gather.7.cloned.1.call-update) | async-done | bytes 4096016 | tf_op jit(solution)/shard_map/all_gather | solution.py:266
  1018.8 5.7 reshape.267
  1024.5 5.5 copy.130
  1030.0 5.5 gather_fusion
  1035.5 5.6 bitcast_select_fusion
  1041.2 6.0 all-to-all-start
  1047.2 109.0 %all-to-all-done = f32[80,8,5,320]{3,0,2,1:T(8,128)} async-done(((f32[80,8,5,320]{3,0,2,1:T(8,128)}), f32[80,8,5,320]{3,0,2,1:T(8,128)}, u32[]{:S(2)}, u32[]{:S(2)}) %all-to-all-start) | async-done | bytes 4096032 | tf_op jit(solution)/shard_map/all_to_all | solution.py:284
  1156.2 2.8 copy.131
  1159.0 33.4 %fusion.98 = f32[5,320,640]{2,1,0:T(8,128)S(1)} fusion(f32[640,5,320]{2,0,1:T(8,128)S(1)} %bitcast.91, f32[5,640,640]{2,1,0:T(8,128)} %param.28), kind=kOutput, calls=%fused_computation.186 | convolution fusion | flops 7864320000 | bytes 16384000 | tf_op jit(solution)/shard_map/kdi,dkc->kic/dot_general | solution.py:288
  1192.4 18.5 %broadcast_select_fusion = (f32[5,640,320]{1,2,0:T(8,128)}, f32[5,640,320]{1,2,0:T(8,128)}, f32[5,640,320]{1,2,0:T(8,128)}) fusion(pred[5]{0:T(512)(128)(4,1)S(1)} %dynamic_slice.26, f32[5,640,320]{1,2,0:T(8,128)} %param.27, f32[5,640,320]{1,2,0:T(8,128)} %param.26, f32[5,320,640]{2,1,0:T(8,128)S(1)} %fusion.98, f32[5,320,320]{2,1,0:T(8,128)S(1)} %copy-done), kind=kOutput, calls=%fused_computation.62 | convolution fusion | flops 3940352000 | bytes 26624004 | tf_op jit(solution)/shard_map/kic,kcj->kij/dot_general | solution.py:289
  1210.9 19.0 %fusion.21 = f32[5,640,320]{1,2,0:T(8,128)S(1)} fusion(f32[5,320,320]{2,1,0:T(8,128)S(1)} %copy-done, f32[5,640,320]{1,2,0:T(8,128)} %get-tuple-element.114, f32[5,640,320]{1,2,0:T(8,128)} %param.26, f32[5,640,320]{1,2,0:T(8,128)} %param.27), kind=kOutput, calls=%fused_computation.43 | convolution fusion | flops 3942400000 | bytes 18432000 | tf_op jit(solution)/shard_map/kij,klj->kil/dot_general | solution.py:293
  1230.0 20.0 %convolution_bitcast_fusion.1 = f32[640,5,320]{0,2,1:T(8,128)} fusion(f32[5,640,320]{1,2,0:T(8,128)S(1)} %fusion.21, f32[5,640,640]{2,1,0:T(8,128)S(1)} %bitcast.89), kind=kOutput, calls=%fused_computation.59 | convolution fusion | flops 7864320000 | bytes 16384000 | tf_op jit(solution)/shard_map/kdi,kil->dkl/dot_general | solution.py:294
  1249.9 6.6 copy.134
  1256.5 4.9 copy.135
  1261.4 4.7 all-to-all-start.1
  1267.9 7.3 fusion.47
  1277.7 116.8 %all-reduce.1 = (f32[4]{0:T(128)S(1)}, f32[5]{0:T(128)S(1)}) all-reduce(f32[4]{0:T(128)S(1)} %get-tuple-element.77, f32[5]{0:T(128)S(1)} %pad_maximum_fusion.3), channel_id=1, replica_groups=mesh['dp'=4,'fsdp'=8] {'dp','fsdp'}, use_global_device_ids=true, to_apply=%region_33.35 | all-reduce | flops 9 | bytes 72 | tf_op jit(solution)/shard_map/psum | solution.py:187
  1396.3 3.2 fusion.86
  1408.0 2.2 concatenate.28
  1410.2 14.4 all-reduce
  1426.1 61.2 %reduce-scatter.9.cloned.1.call-done = f32[80,4]{1,0:T(8,128)} async-done(((f32[640,4]{1,0:T(8,128)}), f32[80,4]{1,0:T(8,128)}) %reduce-scatter.9.cloned.1.call-update) | async-done | bytes 1296 | tf_op jit(solution)/shard_map/reduce_scatter | solution.py:263
  1488.1 5.5 all-gather.1
  1494.3 5.5 gather_fusion.1
  1499.8 3.0 bitcast_multiply_fusion
  1502.8 3.7 copy.136
  1506.5 5.5 mul.302
  1512.0 6.7 fusion.88
  1518.7 2.0 copy.163
  (199 shorter events, 45.1 us)
Async XLA Ops:
  7.2 1185.2 %copy-start = (f32[5,320,320]{2,1,0:T(8,128)S(1)}, f32[5,320,320]{2,1,0:T(8,128)}, u32[]{:S(2)}) copy-start(f32[5,320,320]{2,1,0:T(8,128)} %param.29) | copy-start | bytes 6144004
  7.2 236.5 %copy-start.35 = (f32[80,16]{0,1:T(8,128)S(1)}, f32[80,16]{0,1:T(8,128)}, u32[]{:S(2)}) copy-start(f32[80,16]{0,1:T(8,128)} %param.22) | copy-start | bytes 15364
  7.2 367.5 %copy-start.4 = (bf16[256,640]{1,0:T(8,128)(2,1)S(1)}, bf16[256,640]{1,0:T(8,128)(2,1)}, u32[]{:S(2)}) copy-start(bf16[256,640]{1,0:T(8,128)(2,1)} %param.16) | copy-start | bytes 983044
  7.2 527.2 %all-gather.5.cloned.1.call-start = ((), (), s32[]{:S(2)}) async-start(), calls=%async_computation.5 | async-start | bytes 18432000 | tf_op jit(solution)/shard_map/all_gather | solution.py:196
  11.1 50.8 %collective-permute-start = (bf16[80,12800]{1,0:T(8,128)(2,1)}, bf16[80,12800]{1,0:T(8,128)(2,1)S(1)}, u32[]{:S(2)}, u32[]{:S(2)}) collective-permute-start(bf16[80,12800]{1,0:T(8,128)(2,1)} %convert_element_type.121), channel_id=1, source_target_pairs={{0,1},{1,2},{2,3},{3,4},{4,5},{5,6},{6,7},{7,0},{8,9},{9,10},{10,1... | collective-permute-start | bytes 6144008 | tf_op jit(solution)/shard_map/ppermute | solution.py:24
  61.9 1.3 copy-start.5
  63.2 87.4 %collective-permute-start.1 = (bf16[80,12800]{1,0:T(8,128)(2,1)S(1)}, bf16[80,12800]{1,0:T(8,128)(2,1)S(1)}, u32[]{:S(2)}, u32[]{:S(2)}) collective-permute-start(bf16[80,12800]{1,0:T(8,128)(2,1)S(1)} %collective-permute-done), channel_id=1, source_target_pairs={{0,1},{1,2},{2,3},{3,4},{4,5},{5,6},{6,7},{7,0},{8,9},{9,10},{10,1... | collective-permute-start | bytes 6144008 | tf_op jit(solution)/shard_map/ppermute | solution.py:24
  63.2 91.2 %collective-permute-start.4 = (bf16[80,12800]{1,0:T(8,128)(2,1)}, bf16[80,12800]{1,0:T(8,128)(2,1)}, u32[]{:S(2)}, u32[]{:S(2)}) collective-permute-start(bf16[80,12800]{1,0:T(8,128)(2,1)} %convert_element_type.121), channel_id=1, source_target_pairs={{0,7},{1,0},{2,1},{3,2},{4,3},{5,4},{6,5},{7,6},{8,15},{9,8},{10,9... | collective-permute-start | bytes 6144008 | tf_op jit(solution)/shard_map/ppermute | solution.py:26
  150.6 1.3 copy-start.7
  151.9 89.1 %collective-permute-start.2 = (bf16[80,12800]{1,0:T(8,128)(2,1)S(1)}, bf16[80,12800]{1,0:T(8,128)(2,1)}, u32[]{:S(2)}, u32[]{:S(2)}) collective-permute-start(bf16[80,12800]{1,0:T(8,128)(2,1)S(1)} %collective-permute-done.1), channel_id=1, source_target_pairs={{0,1},{1,2},{2,3},{3,4},{4,5},{5,6},{6,7},{7,0},{8,9},{9,10},{10,1... | collective-permute-start | bytes 6144008 | tf_op jit(solution)/shard_map/ppermute | solution.py:24
  154.4 220.7 %collective-permute-start.5 = (bf16[80,12800]{1,0:T(8,128)(2,1)}, bf16[80,12800]{1,0:T(8,128)(2,1)}, u32[]{:S(2)}, u32[]{:S(2)}) collective-permute-start(bf16[80,12800]{1,0:T(8,128)(2,1)} %collective-permute-done.4), channel_id=1, source_target_pairs={{0,7},{1,0},{2,1},{3,2},{4,3},{5,4},{6,5},{7,6},{8,15},{9,8},{10,9... | collective-permute-start | bytes 6144008 | tf_op jit(solution)/shard_map/ppermute | solution.py:26
  241.0 134.2 %collective-permute-start.3 = (bf16[80,12800]{1,0:T(8,128)(2,1)}, bf16[80,12800]{1,0:T(8,128)(2,1)}, u32[]{:S(2)}, u32[]{:S(2)}) collective-permute-start(bf16[80,12800]{1,0:T(8,128)(2,1)} %collective-permute-done.2), channel_id=1, source_target_pairs={{0,1},{1,2},{2,3},{3,4},{4,5},{5,6},{6,7},{7,0},{8,9},{9,10},{10,1... | collective-permute-start | bytes 6144008 | tf_op jit(solution)/shard_map/ppermute | solution.py:24
  243.6 591.7 %reduce-scatter.5.cloned.1.call-start = ((), (), s32[]{:S(2)}) async-start(), calls=%async_computation.6 | async-start | bytes 40960000 | tf_op jit(solution)/shard_map/reduce_scatter | solution.py:258
  374.1 7.5 copy-start.8
  375.1 7.9 copy-start.37
  375.1 7.9 copy-start.6
  375.1 82.3 %collective-permute-start.6 = (bf16[80,12800]{1,0:T(8,128)(2,1)}, bf16[80,12800]{1,0:T(8,128)(2,1)S(1)}, u32[]{:S(2)}, u32[]{:S(2)}) collective-permute-start(bf16[80,12800]{1,0:T(8,128)(2,1)} %collective-permute-done.5), channel_id=1, source_target_pairs={{0,7},{1,0},{2,1},{3,2},{4,3},{5,4},{6,5},{7,6},{8,15},{9,8},{10,9... | collective-permute-start | bytes 6144008 | tf_op jit(solution)/shard_map/ppermute | solution.py:26
  378.4 6.1 copy-start.2
  481.7 3.1 copy-start.18
  483.0 1.9 copy-start.20
  483.0 1.9 copy-start.28
  483.9 2.3 copy-start.1
  486.2 2.3 copy-start.30
  488.5 19.9 %copy-start.22 = (bf16[256,640]{1,0:T(8,128)(2,1)S(1)}, bf16[256,640]{1,0:T(8,128)(2,1)}, u32[]{:S(2)}) copy-start(bf16[256,640]{1,0:T(8,128)(2,1)} %param.17) | copy-start | bytes 983044
  506.9 1.5 copy-start.27
  544.0 6.2 copy-start.25
  544.1 7.4 copy-start.23
  550.6 0.8 copy-start.9
  551.6 0.7 copy-start.32
  556.5 3.7 copy-start.13
  556.5 3.7 copy-start.29
  556.5 7.8 slice-start
  560.3 14.4 copy-start.11
  560.3 4.1 slice-start.1
  564.4 1.4 copy-start.19
  564.4 2.5 copy-start.21
  565.8 1.7 copy-start.26
  566.9 7.8 copy-start.14
  567.6 7.1 copy-start.16
  567.6 6.7 copy-start.31
  567.6 6.7 copy-start.33
  599.6 384.7 %copy-start.45 = (s32[40]{0:T(128)S(1)}, s32[40]{0:T(128)}, u32[]{:S(2)}) copy-start(s32[40]{0:T(128)} %param.25) | copy-start | bytes 484
  599.6 384.7 %reduce-scatter.7.cloned.1.call-start = ((), (), s32[]{:S(2)}) async-start(), calls=%async_computation.7 | async-start | bytes 9216000 | tf_op jit(solution)/shard_map/reduce_scatter | solution.py:262
  835.3 183.4 %all-gather.7.cloned.1.call-start = ((), (), s32[]{:S(2)}) async-start(), calls=%async_computation.8 | async-start | bytes 5120000 | tf_op jit(solution)/shard_map/all_gather | solution.py:266
  1041.2 115.0 %all-to-all-start = ((f32[80,8,5,320]{3,0,2,1:T(8,128)}), f32[80,8,5,320]{3,0,2,1:T(8,128)}, u32[]{:S(2)}, u32[]{:S(2)}) async-start(f32[80,8,5,320]{3,0,2,1:T(8,128)} %bitcast.90), calls=%async_computation.3 | async-start | bytes 9830400 | tf_op jit(solution)/shard_map/all_to_all | solution.py:284
  1159.0 70.9 %slice-start.2 = ((s8[8192000]{0:T(1024)(128)(4,1)}), s8[4194304]{0:T(1024)(128)(4,1)S(1)}, s32[]{:S(2)}) async-start(s8[8192000]{0:T(1024)(128)(4,1)} %bitcast.88), calls=%async_computation.12 | async-start | bytes 8388608
  1192.4 37.6 %slice-start.3 = ((s8[8192000]{0:T(1024)(128)(4,1)}), s8[3997696]{0:T(1024)(128)(4,1)S(1)}, s32[]{:S(2)}) async-start(s8[8192000]{0:T(1024)(128)(4,1)} %bitcast.88), calls=%async_computation.13 | async-start | bytes 7995392
  1261.4 5.1 copy-start.42
  1261.4 5.1 copy-start.46
  1261.4 6.4 copy-start.44
  1261.4 232.8 %all-to-all-start.1 = ((f32[8,80,5,320]{3,1,2,0:T(8,128)}), f32[8,80,5,320]{3,1,2,0:T(8,128)}, u32[]{:S(2)}, u32[]{:S(2)}) async-start(f32[8,80,5,320]{3,1,2,0:T(8,128)} %copy.135), calls=%async_computation.4 | async-start | bytes 9830400 | tf_op jit(solution)/shard_map/all_to_all | solution.py:297
  1266.2 221.1 %reduce-scatter.9.cloned.1.call-start = ((), (), s32[]{:S(2)}) async-start(), calls=%async_computation.9 | async-start | bytes 368640 | tf_op jit(solution)/shard_map/reduce_scatter | solution.py:263
  1267.8 8.1 copy-start.41
  1267.8 8.3 copy-start.43
  1275.9 123.6 %copy-start.38 = (f32[256]{0:T(256)S(1)}, f32[256]{0:T(256)}, u32[]{:S(2)}) copy-start(f32[256]{0:T(256)} %copy-done.37) | copy-start | bytes 3076
  1275.9 125.8 %copy-start.12 = (bf16[20,32,256]{2,1,0:T(8,128)(2,1)S(1)}, bf16[20,32,256]{2,1,0:T(8,128)(2,1)}, u32[]{:S(2)}) copy-start(bf16[20,32,256]{2,1,0:T(8,128)(2,1)} %copy-done.11) | copy-start | bytes 983044
  1275.9 125.8 %copy-start.15 = (bf16[20,32,256]{2,1,0:T(8,128)(2,1)S(1)}, bf16[20,32,256]{2,1,0:T(8,128)(2,1)}, u32[]{:S(2)}) copy-start(bf16[20,32,256]{2,1,0:T(8,128)(2,1)} %copy-done.14) | copy-start | bytes 983044
  1396.2 5.5 copy-start.17
  1396.3 9.5 copy-start.10
  1396.3 9.5 copy-start.24
  1401.7 91.9 %copy-start.36 = (f32[80,16]{0,1:T(8,128)S(1)}, f32[80,16]{0,1:T(8,128)}, u32[]{:S(2)}) copy-start(f32[80,16]{0,1:T(8,128)} %param.22) | copy-start | bytes 15364
  1401.7 91.9 %copy-start.39 = (f32[80,16]{0,1:T(8,128)S(1)}, f32[80,16]{0,1:T(8,128)}, u32[]{:S(2)}) copy-start(f32[80,16]{0,1:T(8,128)} %param.23) | copy-start | bytes 15364
  1401.7 91.9 %copy-start.40 = (f32[80,16]{0,1:T(8,128)S(1)}, f32[80,16]{0,1:T(8,128)}, u32[]{:S(2)}) copy-start(f32[80,16]{0,1:T(8,128)} %param.24) | copy-start | bytes 15364
  1512.0 6.7 copy-start.3
  (1 other events, 0.7 us)
Sparse Core Ops, SparseCore 0:
  243.7 290.6 all-gather.4
  599.7 235.5 reduce-scatter.4
  839.0 145.2 reduce-scatter.6
  985.7 32.9 all-gather.6
  1425.7 61.5 reduce-scatter.8
